TPU v7x, 256 devices: a whole 4x4x8 slice. The times are simulated.
256 devices in a mesh: row: 4 (over y), col: 16 (over z_hi, x, core), dep: 4 (over z_lo).
Axes of the slice: x: 4, y: 4, z: 8 (z_hi: 2, z_lo: 4; z = z_hi * 4 + z_lo), core: 2. Of those that a mesh axis runs over, the one named last changes fastest.
Arguments:
- grad_out: bfloat16 [4, 512, 12288], P('row', 'dep', 'col'), may hold values from -7 to 7
- out_weight: bfloat16 [8192, 12288], P('row', 'col'), may hold values from -0.09375 to 0.09375
- query_rows: bfloat16 [2048, 8192], P('dep', ('row', 'col')), may hold values from -6 to 6
- key_rows: bfloat16 [2048, 8192], P('dep', ('row', 'col')), may hold values from -6 to 6
- value_rows: bfloat16 [2048, 8192], P('dep', ('row', 'col')), may hold values from -7 to 7
- seg_lengths: int32 [8], replicated, may hold values from 1 to 1536, 2048 in all
Outputs:
- grad_weight: float32 [8192, 12288], P('row', 'col')
- grad_query: bfloat16 [2048, 8192], P('dep', ('row', 'col'))
- grad_key: bfloat16 [2048, 8192], P('dep', ('row', 'col'))
- grad_value: bfloat16 [2048, 8192], P('dep', ('row', 'col'))
All inputs are finite; a program needn't handle non-finite values.
Results may differ from a plain program's by a relative error of at most 0.029.
Values may be sent and summed in bfloat16 or wider, within the bound.
No kernel may reach another device: no remote copies, remote signals or barrier semaphores. Data moves between devices by JAX's collectives and lax.ppermute only.
A program may use at most 128 MiB of HBM per device.

v0:
```python
import math
import jax
import jax.numpy as jnp
from jax import lax
from jax.sharding import Mesh
from jax.sharding import PartitionSpec as P

NEG_FILL = -1e30
FAR = 1 << 30
COL = ("zh", "x", "core")
DEP = "zl"


def segment_count(positions, seg_ends):
    return jnp.sum((positions[:, None] >= seg_ends[None, :]).astype(jnp.int32), axis=1)


def shift(x, axis, n, s):
    return lax.ppermute(x, axis, [(i, (i + s) % n) for i in range(n)])


def shift_open(x, axis, n, s):
    return lax.ppermute(x, axis, [(i, i + s) for i in range(n) if 0 <= i + s < n])


def roll_rows(x, amount, axis):
    size = x.shape[axis]
    doubled = jnp.concatenate([x, x], axis=axis)
    return lax.dynamic_slice_in_dim(doubled, (size - amount) % size, size, axis=axis)


def rolled_gather(x, axis, n, stack_axis=0):
    parts = [x] + [shift(x, axis, n, -s) for s in range(1, n)]
    return jnp.stack(parts, axis=stack_axis)


def pp_reduce_scatter(x, axis, n, dim):
    me = lax.axis_index(axis)
    acc = lax.dynamic_index_in_dim(x, me, dim, keepdims=False).astype(jnp.float32)
    for s in range(1, n):
        send = lax.dynamic_index_in_dim(x, (me + s) % n, dim, keepdims=False)
        acc = acc + shift(send, axis, n, s).astype(jnp.float32)
    return acc


def make_shards(n_zh, n_x, n_core, n_row, n_dep):

    def shards(grad_out, out_weight, query_rows, key_rows, value_rows, seg_lengths):
        n_tok, feat = (grad_out.shape[1], grad_out.shape[2])
        tok_depth = n_row * n_tok
        head_dim = query_rows.shape[1]
        inv_root = 1.0 / math.sqrt(head_dim)
        me_r = lax.axis_index("row")
        me_d = lax.axis_index(DEP)
        local = grad_out[0]
        grad_rows = rolled_gather(local, "row", n_row).reshape(tok_depth, feat)
        partial = jnp.einsum(
            "hf,tf->ht", out_weight, grad_rows, preferred_element_type=jnp.float32
        ).astype(jnp.bfloat16)
        partial = partial.reshape(n_zh, n_x, n_core, head_dim, tok_depth)
        partial = pp_reduce_scatter(partial, "core", n_core, 2).astype(jnp.bfloat16)
        partial = pp_reduce_scatter(partial, "x", n_x, 1).astype(jnp.bfloat16)
        partial = pp_reduce_scatter(partial, "zh", n_zh, 0).astype(jnp.bfloat16)
        context_grad = roll_rows(partial.T, me_r * n_tok, 0)
        kv = jnp.concatenate([key_rows, value_rows], axis=1)
        kv_all = jnp.stack(
            [kv] + [shift_open(kv, DEP, n_dep, s) for s in range(1, n_dep)], axis=0
        ).reshape(n_dep * tok_depth, 2 * head_dim)
        keys_all, values_all = (kv_all[:, :head_dim], kv_all[:, head_dim:])
        src_depth = me_d - jnp.arange(n_dep, dtype=jnp.int32)
        key_pos = (
            jnp.where(src_depth >= 0, src_depth * tok_depth, FAR)[:, None]
            + jnp.arange(tok_depth, dtype=jnp.int32)[None, :]
        ).reshape(-1)
        seg_ends = jnp.cumsum(seg_lengths)
        key_seg = segment_count(key_pos, seg_ends)
        query_pos = me_d * tok_depth + jnp.arange(tok_depth, dtype=jnp.int32)
        query_seg = segment_count(query_pos, seg_ends)
        allowed = (query_seg[:, None] == key_seg[None, :]) & (
            key_pos[None, :] <= query_pos[:, None]
        )
        scores = (
            jnp.einsum("qh,kh->qk", query_rows, keys_all, preferred_element_type=jnp.float32)
            * inv_root
        )
        masked = jnp.where(allowed, scores, NEG_FILL)
        row_max = jnp.max(masked, axis=1, keepdims=True)
        exponent = jnp.where(allowed, jnp.exp(masked - row_max), 0.0)
        row_sum = jnp.sum(exponent, axis=1, keepdims=True)
        prob_full = exponent / row_sum
        prob_half = prob_full.astype(jnp.bfloat16)
        context = jnp.dot(prob_half, values_all, preferred_element_type=jnp.float32).astype(
            jnp.bfloat16
        )
        context = roll_rows(context, -me_r * n_tok, 0)
        ctx_all = lax.all_gather(context[None], COL + (DEP,), axis=0, tiled=True)
        ctx_all = ctx_all.reshape(n_zh * n_x * n_core, n_dep * tok_depth, head_dim)
        grad_prob = jnp.dot(context_grad, values_all.T, preferred_element_type=jnp.float32)
        delta_row = jnp.sum(prob_full * grad_prob, axis=1, keepdims=True)
        grad_score = (prob_full * (grad_prob - delta_row)).astype(jnp.bfloat16)
        grad_query = (
            jnp.dot(grad_score, keys_all, preferred_element_type=jnp.float32) * inv_root
        ).astype(jnp.bfloat16)
        key_partial = (
            jnp.einsum("qk,qh->kh", grad_score, query_rows, preferred_element_type=jnp.float32)
            * inv_root
        ).astype(jnp.bfloat16)
        value_partial = jnp.einsum(
            "qk,qh->kh", prob_half, context_grad, preferred_element_type=jnp.float32
        ).astype(jnp.bfloat16)
        kv_partial = jnp.concatenate([key_partial, value_partial], axis=1).reshape(
            n_dep, tok_depth, 2 * head_dim
        )
        kv_grad = kv_partial[0].astype(jnp.float32)
        for s in range(1, n_dep):
            kv_grad = kv_grad + shift_open(kv_partial[s], DEP, n_dep, -s).astype(jnp.float32)
        kv_grad = kv_grad.astype(jnp.bfloat16)
        grad_key, grad_value = (kv_grad[:, :head_dim], kv_grad[:, head_dim:])
        by_depth = roll_rows(rolled_gather(local, DEP, n_dep), me_d, 0)
        rows_all = rolled_gather(by_depth, "row", n_row, stack_axis=1)
        rows_all = rows_all.reshape(n_dep * tok_depth, feat)
        grad_weight = jnp.einsum(
            "ntk,tf->nkf", ctx_all, rows_all, preferred_element_type=jnp.float32
        ).reshape(n_zh * n_x * n_core * head_dim, feat)
        return (grad_weight, grad_query, grad_key, grad_value)

    return shards


def solution(mesh):
    n_row, n_col, n_dep = (mesh.shape["row"], mesh.shape["col"], mesh.shape["dep"])
    n_zh, n_core = (2, 2)
    n_x = n_col // (n_zh * n_core)
    fine = Mesh(mesh.devices.reshape(n_row, n_zh, n_x, n_core, n_dep), ("row",) + COL + (DEP,))
    in_specs = (
        P("row", DEP, COL),
        P("row", COL),
        P(DEP, ("row",) + COL),
        P(DEP, ("row",) + COL),
        P(DEP, ("row",) + COL),
        P(),
    )
    out_specs = (
        P("row", COL),
        P(DEP, ("row",) + COL),
        P(DEP, ("row",) + COL),
        P(DEP, ("row",) + COL),
    )
    return jax.shard_map(
        make_shards(n_zh, n_x, n_core, n_row, n_dep),
        mesh=fine,
        in_specs=in_specs,
        out_specs=out_specs,
        check_vma=False,
    )
```

profile of v0, /device:TPU:96, one launch (start us, length us, event | category | flops | bytes accessed | tf_op | source)
XLA Modules:
  0.0 337.7 jit_solution(12385850366455091268)
XLA Ops:
  7.2 3.1 collective-permute-start.9
  11.9 7.1 %collective-permute-done.9 = bf16[128,768]{1,0:T(8,128)(2,1)S(1)} collective-permute-done((bf16[128,768]{1,0:T(8,128)(2,1)}, bf16[128,768]{1,0:T(8,128)(2,1)S(1)}, u32[]{:S(2)}, u32[]{:S(2)}) %collective-permute-start.9) | collective-permute-done | bytes 196640 | tf_op jit(solution)/shard_map/ppermute | solution.py:19
  23.8 3.1 fusion.1
  27.0 3.2 reshape.113
  30.2 6.3 %constant_dynamic-slice_fusion.1 = (bf16[2,4,1,128,512]{3,2,1,0,4:T(2,128)(2,1)}, bf16[2,4,1,128,512]{3,2,1,0,4:T(2,128)(2,1)}) fusion(bf16[2,4,2,128,512]{3,2,1,0,4:T(2,128)(2,1)S(1)} %reshape.113, s32[]{:T(128)S(6)} %select_n.93, s32[]{:T(128)S(6)} %select_n.95), kind=kLoop, calls=%fused_computation.71 | loop fusion | bytes 4194312 | tf_op jit(solution)/shard_map/jit(dynamic_index_in_dim)/dynamic_slice | solution.py:39
  36.6 6.0 %copy.34 = bf16[2,4,1,128,512]{4,3,1,0,2:T(8,128)(2,1)} copy(bf16[2,4,1,128,512]{3,2,1,0,4:T(2,128)(2,1)} %get-tuple-element.19) | data formatting | bytes 2097152
  50.3 3.1 collective-permute-done
  53.4 16.4 %collective-permute-done.1 = bf16[512,256]{1,0:T(8,128)(2,1)} collective-permute-done((bf16[512,256]{1,0:T(8,128)(2,1)S(1)}, bf16[512,256]{1,0:T(8,128)(2,1)}, u32[]{:S(2)}, u32[]{:S(2)}) %collective-permute-start.1) | collective-permute-done | bytes 262176 | tf_op jit(solution)/shard_map/ppermute | solution.py:23
  82.6 6.3 %collective-permute-done.14 = bf16[2,128,512]{2,1,0:T(8,128)(2,1)S(1)} collective-permute-done((bf16[2,128,512]{2,1,0:T(8,128)(2,1)S(1)}, bf16[2,128,512]{2,1,0:T(8,128)(2,1)S(1)}, u32[]{:S(2)}, u32[]{:S(2)}) %collective-permute-start.14) | collective-permute-done | bytes 262176 | tf_op jit(solution)/shard_map/ppermute | solution.py:19
  89.1 5.5 %collective-permute-start.16 = (bf16[128,512]{1,0:T(8,128)(2,1)S(1)}, bf16[128,512]{1,0:T(8,128)(2,1)S(1)}, u32[]{:S(2)}, u32[]{:S(2)}) collective-permute-start(bf16[128,512]{1,0:T(8,128)(2,1)S(1)} %dynamic-slice_bitcast_fusion.3), channel_id=1, source_target_pairs={{0,32},{32,0},{1,33},{33,1},{2,34},{34,2},{3,35},{35,3},{4,36},{36... | collective-permute-start | bytes 393224 | tf_op jit(solution)/shard_map/ppermute | solution.py:19
  96.3 3.9 %collective-permute-done.16 = bf16[128,512]{1,0:T(8,128)(2,1)S(1)} collective-permute-done((bf16[128,512]{1,0:T(8,128)(2,1)S(1)}, bf16[128,512]{1,0:T(8,128)(2,1)S(1)}, u32[]{:S(2)}, u32[]{:S(2)}) %collective-permute-start.16) | collective-permute-done | bytes 131104 | tf_op jit(solution)/shard_map/ppermute | solution.py:19
  100.2 4.0 %multiply_reduce_fusion = (f32[512]{0:T(512)S(1)}, f32[512,2048]{0,1:T(8,128)S(1)}, f32[512,2048]{0,1:T(8,128)}) fusion(f32[512]{0:T(512)S(1)} %fusion.4, f32[512]{0:T(512)S(1)} %get-tuple-element.28, f32[2048,512]{1,0:T(8,128)S(1)} %get-tuple-element.29, s32[512]{0:T(512)S(1)} %copy-done.13, s32[2048]{0:T(1024)S(1)} %bitcast.104, ...), kind=kOutput, calls=%fused_computation.2 | convolution fusion | flops 279182848 | bytes 13264900 | tf_op jit(solution)/shard_map/dot_general | solution.py:98
  107.6 3.7 %collective-permute-start.5 = (bf16[128,768]{1,0:T(8,128)(2,1)S(1)}, bf16[128,768]{1,0:T(8,128)(2,1)S(1)}, u32[]{:S(2)}, u32[]{:S(2)}) collective-permute-start(bf16[128,768]{1,0:T(8,128)(2,1)S(1)} %bitcast.93), channel_id=1, source_target_pairs={{0,1},{1,2},{2,3},{3,0},{4,5},{5,6},{6,7},{7,4},{8,9},{9,10},{10,1... | collective-permute-start | bytes 589832 | tf_op jit(solution)/shard_map/ppermute | solution.py:19
  111.3 4.9 %collective-permute-done.3 = bf16[128,768]{1,0:T(8,128)(2,1)S(1)} collective-permute-done((bf16[128,768]{1,0:T(8,128)(2,1)S(1)}, bf16[128,768]{1,0:T(8,128)(2,1)S(1)}, u32[]{:S(2)}, u32[]{:S(2)}) %collective-permute-start.3) | collective-permute-done | bytes 196640 | tf_op jit(solution)/shard_map/ppermute | solution.py:19
  116.2 5.0 %collective-permute-done.4 = bf16[128,768]{1,0:T(8,128)(2,1)S(1)} collective-permute-done((bf16[128,768]{1,0:T(8,128)(2,1)S(1)}, bf16[128,768]{1,0:T(8,128)(2,1)S(1)}, u32[]{:S(2)}, u32[]{:S(2)}) %collective-permute-start.4) | collective-permute-done | bytes 196640 | tf_op jit(solution)/shard_map/ppermute | solution.py:19
  123.6 18.4 %collective-permute-done.6 = bf16[4,128,768]{2,1,0:T(8,128)(2,1)S(1)} collective-permute-done((bf16[4,128,768]{2,1,0:T(8,128)(2,1)S(1)}, bf16[4,128,768]{2,1,0:T(8,128)(2,1)S(1)}, u32[]{:S(2)}, u32[]{:S(2)}) %collective-permute-start.6) | collective-permute-done | bytes 786464 | tf_op jit(solution)/shard_map/ppermute | solution.py:19
  143.9 13.0 %collective-permute-done.8 = bf16[4,128,768]{2,1,0:T(8,128)(2,1)S(1)} collective-permute-done((bf16[4,128,768]{2,1,0:T(8,128)(2,1)S(1)}, bf16[4,128,768]{2,1,0:T(8,128)(2,1)S(1)}, u32[]{:S(2)}, u32[]{:S(2)}) %collective-permute-start.8) | collective-permute-done | bytes 786464 | tf_op jit(solution)/shard_map/ppermute | solution.py:19
  163.1 7.6 %collective-permute-start.17 = (bf16[512,256]{0,1:T(8,128)(2,1)S(1)}, bf16[512,256]{0,1:T(8,128)(2,1)S(1)}, u32[]{:S(2)}, u32[]{:S(2)}) collective-permute-start(bf16[512,256]{0,1:T(8,128)(2,1)S(1)} %get-tuple-element.20), channel_id=1, source_target_pairs={{1,0},{2,1},{3,2},{5,4},{6,5},{7,6},{9,8},{10,9},{11,10},{13,12},{... | collective-permute-start | bytes 786440 | tf_op jit(solution)/shard_map/ppermute | solution.py:23
  175.1 3.9 %collective-permute-done.17 = bf16[512,256]{0,1:T(8,128)(2,1)S(1)} collective-permute-done((bf16[512,256]{0,1:T(8,128)(2,1)S(1)}, bf16[512,256]{0,1:T(8,128)(2,1)S(1)}, u32[]{:S(2)}, u32[]{:S(2)}) %collective-permute-start.17) | collective-permute-done | bytes 262176 | tf_op jit(solution)/shard_map/ppermute | solution.py:23
  179.0 7.4 %collective-permute-done.18 = bf16[512,256]{0,1:T(8,128)(2,1)S(1)} collective-permute-done((bf16[512,256]{0,1:T(8,128)(2,1)S(1)}, bf16[512,256]{0,1:T(8,128)(2,1)S(1)}, u32[]{:S(2)}, u32[]{:S(2)}) %collective-permute-start.18) | collective-permute-done | bytes 262176 | tf_op jit(solution)/shard_map/ppermute | solution.py:23
  186.3 6.2 %collective-permute-done.19 = bf16[512,256]{0,1:T(8,128)(2,1)S(1)} collective-permute-done((bf16[512,256]{0,1:T(8,128)(2,1)S(1)}, bf16[512,256]{0,1:T(8,128)(2,1)S(1)}, u32[]{:S(2)}, u32[]{:S(2)}) %collective-permute-start.19) | collective-permute-done | bytes 262176 | tf_op jit(solution)/shard_map/ppermute | solution.py:23
  194.2 112.5 %all-gather.3.cloned.1.call-done = bf16[32768,128]{1,0:T(8,128)(2,1)} async-done(((bf16[512,128]{1,0:T(8,128)(2,1)}), bf16[32768,128]{1,0:T(8,128)(2,1)}) %all-gather.3.cloned.1.call-update) | async-done | bytes 8388624 | tf_op jit(solution)/shard_map/all_gather | solution.py:96
  306.7 12.4 %copy.23 = bf16[16,2048,128]{1,2,0:T(8,128)(2,1)} copy(bf16[16,2048,128]{2,1,0:T(8,128)(2,1)} %bitcast.81) | data formatting | bytes 16777216 | tf_op jit(solution)/shard_map/reshape | solution.py:97
  319.0 11.8 %fusion.29 = f32[2048,768]{1,0:T(8,128)} fusion(bf16[2048,2048]{1,0:T(8,128)(2,1)} %bitcast.82, bf16[2048,768]{1,0:T(8,128)(2,1)} %bitcast.83), kind=kOutput, calls=%fused_computation.76 | convolution fusion | flops 6442450944 | bytes 17825792 | tf_op jit(solution)/shard_map/ntk,tf->nkf/dot_general | solution.py:122
  (99 shorter events, 48.6 us)
Async XLA Ops:
  7.2 299.5 %all-gather.3.cloned.1.call-start = ((), (), s32[]{:S(2)}) async-start(), calls=%async_computation | async-start | bytes 8519680 | tf_op jit(solution)/shard_map/all_gather | solution.py:96
  7.2 11.8 %collective-permute-start.9 = (bf16[128,768]{1,0:T(8,128)(2,1)}, bf16[128,768]{1,0:T(8,128)(2,1)S(1)}, u32[]{:S(2)}, u32[]{:S(2)}) collective-permute-start(bf16[128,768]{1,0:T(8,128)(2,1)} %bitcast.88), channel_id=1, source_target_pairs={{0,192},{64,0},{128,64},{192,128},{1,193},{65,1},{129,65},{193,129... | collective-permute-start | bytes 589832 | tf_op jit(solution)/shard_map/ppermute | solution.py:19
  10.3 9.6 %collective-permute-start.10 = (bf16[128,768]{1,0:T(8,128)(2,1)}, bf16[128,768]{1,0:T(8,128)(2,1)S(1)}, u32[]{:S(2)}, u32[]{:S(2)}) collective-permute-start(bf16[128,768]{1,0:T(8,128)(2,1)} %bitcast.89), channel_id=1, source_target_pairs={{0,128},{64,192},{128,0},{192,64},{1,129},{65,193},{129,1},{193,65... | collective-permute-start | bytes 589832 | tf_op jit(solution)/shard_map/ppermute | solution.py:19
  10.9 11.8 %collective-permute-start.11 = (bf16[128,768]{1,0:T(8,128)(2,1)}, bf16[128,768]{1,0:T(8,128)(2,1)}, u32[]{:S(2)}, u32[]{:S(2)}) collective-permute-start(bf16[128,768]{1,0:T(8,128)(2,1)} %bitcast.90), channel_id=1, source_target_pairs={{0,64},{64,128},{128,192},{192,0},{1,65},{65,129},{129,193},{193,1... | collective-permute-start | bytes 589832 | tf_op jit(solution)/shard_map/ppermute | solution.py:19
  42.5 28.6 %collective-permute-start.12 = (bf16[2,4,128,512]{3,2,1,0:T(8,128)(2,1)}, bf16[2,4,128,512]{3,2,1,0:T(8,128)(2,1)}, u32[]{:S(2)}, u32[]{:S(2)}) collective-permute-start(bf16[2,4,128,512]{3,2,1,0:T(8,128)(2,1)} %bitcast.28), channel_id=1, source_target_pairs={{0,4},{4,0},{1,5},{5,1},{2,6},{6,2},{3,7},{7,3},{8,12},{12,8},{9,1... | collective-permute-start | bytes 3145736 | tf_op jit(solution)/shard_map/ppermute | solution.py:19
  42.6 10.7 %collective-permute-start = (bf16[512,256]{1,0:T(8,128)(2,1)S(1)}, bf16[512,256]{1,0:T(8,128)(2,1)}, u32[]{:S(2)}, u32[]{:S(2)}) collective-permute-start(bf16[512,256]{1,0:T(8,128)(2,1)S(1)} %constant_dynamic-update-slice_fusion), channel_id=1, source_target_pairs={{0,1},{1,2},{2,3},{4,5},{5,6},{6,7},{8,9},{9,10},{10,11},{12,13},{... | collective-permute-start | bytes 786440 | tf_op jit(solution)/shard_map/ppermute | solution.py:23
  43.9 25.8 %collective-permute-start.1 = (bf16[512,256]{1,0:T(8,128)(2,1)S(1)}, bf16[512,256]{1,0:T(8,128)(2,1)}, u32[]{:S(2)}, u32[]{:S(2)}) collective-permute-start(bf16[512,256]{1,0:T(8,128)(2,1)S(1)} %constant_dynamic-update-slice_fusion), channel_id=1, source_target_pairs={{0,2},{1,3},{4,6},{5,7},{8,10},{9,11},{12,14},{13,15},{16,18},{17,... | collective-permute-start | bytes 786440 | tf_op jit(solution)/shard_map/ppermute | solution.py:23
  45.2 24.5 %collective-permute-start.2 = (bf16[512,256]{1,0:T(8,128)(2,1)S(1)}, bf16[512,256]{1,0:T(8,128)(2,1)}, u32[]{:S(2)}, u32[]{:S(2)}) collective-permute-start(bf16[512,256]{1,0:T(8,128)(2,1)S(1)} %constant_dynamic-update-slice_fusion), channel_id=1, source_target_pairs={{0,3},{4,7},{8,11},{12,15},{16,19},{20,23},{24,27},{28,31},{32,35}... | collective-permute-start | bytes 786440 | tf_op jit(solution)/shard_map/ppermute | solution.py:23
  46.6 23.1 %copy-start.12 = (s32[512]{0:T(512)}, s32[512]{0:T(512)S(1)}, u32[]{:S(2)}) copy-start(s32[512]{0:T(512)S(1)} %iota_add_fusion) | copy-start | bytes 6148
  71.1 33.1 %copy-start.6 = (bf16[4,512,256]{2,1,0:T(8,128)(2,1)}, bf16[4,512,256]{2,1,0:T(8,128)(2,1)S(1)}, u32[]{:S(2)}) copy-start(bf16[4,512,256]{2,1,0:T(8,128)(2,1)S(1)} %pad_maximum_fusion.1) | copy-start | bytes 3145732
  73.1 9.5 %collective-permute-start.13 = (bf16[2,128,512]{2,1,0:T(8,128)(2,1)S(1)}, bf16[2,128,512]{2,1,0:T(8,128)(2,1)S(1)}, u32[]{:S(2)}, u32[]{:S(2)}) collective-permute-start(bf16[2,128,512]{2,1,0:T(8,128)(2,1)S(1)} %get-tuple-element.23), channel_id=1, source_target_pairs={{0,8},{8,16},{16,24},{24,0},{1,9},{9,17},{17,25},{25,1},{2,10},{10... | collective-permute-start | bytes 786440 | tf_op jit(solution)/shard_map/ppermute | solution.py:19
  74.7 14.2 %collective-permute-start.14 = (bf16[2,128,512]{2,1,0:T(8,128)(2,1)S(1)}, bf16[2,128,512]{2,1,0:T(8,128)(2,1)S(1)}, u32[]{:S(2)}, u32[]{:S(2)}) collective-permute-start(bf16[2,128,512]{2,1,0:T(8,128)(2,1)S(1)} %get-tuple-element.25), channel_id=1, source_target_pairs={{0,16},{8,24},{16,0},{24,8},{1,17},{9,25},{17,1},{25,9},{2,18},{10... | collective-permute-start | bytes 786440 | tf_op jit(solution)/shard_map/ppermute | solution.py:19
  77.4 11.5 %collective-permute-start.15 = (bf16[2,128,512]{2,1,0:T(8,128)(2,1)S(1)}, bf16[2,128,512]{2,1,0:T(8,128)(2,1)S(1)}, u32[]{:S(2)}, u32[]{:S(2)}) collective-permute-start(bf16[2,128,512]{2,1,0:T(8,128)(2,1)S(1)} %get-tuple-element.24), channel_id=1, source_target_pairs={{0,24},{8,0},{16,8},{24,16},{1,25},{9,1},{17,9},{25,17},{2,26},{10... | collective-permute-start | bytes 786440 | tf_op jit(solution)/shard_map/ppermute | solution.py:19
  89.1 11.1 %collective-permute-start.16 = (bf16[128,512]{1,0:T(8,128)(2,1)S(1)}, bf16[128,512]{1,0:T(8,128)(2,1)S(1)}, u32[]{:S(2)}, u32[]{:S(2)}) collective-permute-start(bf16[128,512]{1,0:T(8,128)(2,1)S(1)} %dynamic-slice_bitcast_fusion.3), channel_id=1, source_target_pairs={{0,32},{32,0},{1,33},{33,1},{2,34},{34,2},{3,35},{35,3},{4,36},{36... | collective-permute-start | bytes 393224 | tf_op jit(solution)/shard_map/ppermute | solution.py:19
  107.4 8.8 %collective-permute-start.3 = (bf16[128,768]{1,0:T(8,128)(2,1)S(1)}, bf16[128,768]{1,0:T(8,128)(2,1)S(1)}, u32[]{:S(2)}, u32[]{:S(2)}) collective-permute-start(bf16[128,768]{1,0:T(8,128)(2,1)S(1)} %bitcast.91), channel_id=1, source_target_pairs={{0,3},{1,0},{2,1},{3,2},{4,7},{5,4},{6,5},{7,6},{8,11},{9,8},{10,9... | collective-permute-start | bytes 589832 | tf_op jit(solution)/shard_map/ppermute | solution.py:19
  107.5 13.8 %collective-permute-start.4 = (bf16[128,768]{1,0:T(8,128)(2,1)S(1)}, bf16[128,768]{1,0:T(8,128)(2,1)S(1)}, u32[]{:S(2)}, u32[]{:S(2)}) collective-permute-start(bf16[128,768]{1,0:T(8,128)(2,1)S(1)} %bitcast.92), channel_id=1, source_target_pairs={{0,2},{1,3},{2,0},{3,1},{4,6},{5,7},{6,4},{7,5},{8,10},{9,11},{10,... | collective-permute-start | bytes 589832 | tf_op jit(solution)/shard_map/ppermute | solution.py:19
  107.6 13.7 %collective-permute-start.5 = (bf16[128,768]{1,0:T(8,128)(2,1)S(1)}, bf16[128,768]{1,0:T(8,128)(2,1)S(1)}, u32[]{:S(2)}, u32[]{:S(2)}) collective-permute-start(bf16[128,768]{1,0:T(8,128)(2,1)S(1)} %bitcast.93), channel_id=1, source_target_pairs={{0,1},{1,2},{2,3},{3,0},{4,5},{5,6},{6,7},{7,4},{8,9},{9,10},{10,1... | collective-permute-start | bytes 589832 | tf_op jit(solution)/shard_map/ppermute | solution.py:19
  121.4 37.3 %copy-start.5 = (f32[512,2048]{0,1:T(8,128)S(1)}, f32[512,2048]{0,1:T(8,128)}, u32[]{:S(2)}) copy-start(f32[512,2048]{0,1:T(8,128)} %get-tuple-element.30) | copy-start | bytes 12582916
  121.5 20.6 %collective-permute-start.6 = (bf16[4,128,768]{2,1,0:T(8,128)(2,1)S(1)}, bf16[4,128,768]{2,1,0:T(8,128)(2,1)S(1)}, u32[]{:S(2)}, u32[]{:S(2)}) collective-permute-start(bf16[4,128,768]{2,1,0:T(8,128)(2,1)S(1)} %constant_dynamic-slice_fusion.2), channel_id=1, source_target_pairs={{0,192},{64,0},{128,64},{192,128},{1,193},{65,1},{129,65},{193,129... | collective-permute-start | bytes 2359304 | tf_op jit(solution)/shard_map/ppermute | solution.py:19
  121.9 22.0 %collective-permute-start.7 = (bf16[4,128,768]{2,1,0:T(8,128)(2,1)S(1)}, bf16[4,128,768]{2,1,0:T(8,128)(2,1)S(1)}, u32[]{:S(2)}, u32[]{:S(2)}) collective-permute-start(bf16[4,128,768]{2,1,0:T(8,128)(2,1)S(1)} %constant_dynamic-slice_fusion.2), channel_id=1, source_target_pairs={{0,128},{64,192},{128,0},{192,64},{1,129},{65,193},{129,1},{193,65... | collective-permute-start | bytes 2359304 | tf_op jit(solution)/shard_map/ppermute | solution.py:19
  122.4 34.5 %collective-permute-start.8 = (bf16[4,128,768]{2,1,0:T(8,128)(2,1)S(1)}, bf16[4,128,768]{2,1,0:T(8,128)(2,1)S(1)}, u32[]{:S(2)}, u32[]{:S(2)}) collective-permute-start(bf16[4,128,768]{2,1,0:T(8,128)(2,1)S(1)} %constant_dynamic-slice_fusion.2), channel_id=1, source_target_pairs={{0,64},{64,128},{128,192},{192,0},{1,65},{65,129},{129,193},{193,1... | collective-permute-start | bytes 2359304 | tf_op jit(solution)/shard_map/ppermute | solution.py:19
  163.1 15.8 %collective-permute-start.17 = (bf16[512,256]{0,1:T(8,128)(2,1)S(1)}, bf16[512,256]{0,1:T(8,128)(2,1)S(1)}, u32[]{:S(2)}, u32[]{:S(2)}) collective-permute-start(bf16[512,256]{0,1:T(8,128)(2,1)S(1)} %get-tuple-element.20), channel_id=1, source_target_pairs={{1,0},{2,1},{3,2},{5,4},{6,5},{7,6},{9,8},{10,9},{11,10},{13,12},{... | collective-permute-start | bytes 786440 | tf_op jit(solution)/shard_map/ppermute | solution.py:23
  170.7 15.6 %collective-permute-start.18 = (bf16[512,256]{0,1:T(8,128)(2,1)S(1)}, bf16[512,256]{0,1:T(8,128)(2,1)S(1)}, u32[]{:S(2)}, u32[]{:S(2)}) collective-permute-start(bf16[512,256]{0,1:T(8,128)(2,1)S(1)} %get-tuple-element.22), channel_id=1, source_target_pairs={{2,0},{3,1},{6,4},{7,5},{10,8},{11,9},{14,12},{15,13},{18,16},{19,... | collective-permute-start | bytes 786440 | tf_op jit(solution)/shard_map/ppermute | solution.py:23
  172.1 20.4 %collective-permute-start.19 = (bf16[512,256]{0,1:T(8,128)(2,1)S(1)}, bf16[512,256]{0,1:T(8,128)(2,1)S(1)}, u32[]{:S(2)}, u32[]{:S(2)}) collective-permute-start(bf16[512,256]{0,1:T(8,128)(2,1)S(1)} %get-tuple-element.21), channel_id=1, source_target_pairs={{3,0},{7,4},{11,8},{15,12},{19,16},{23,20},{27,24},{31,28},{35,32}... | collective-permute-start | bytes 786440 | tf_op jit(solution)/shard_map/ppermute | solution.py:23
  (13 other events, 108.8 us)
Sparse Core Ops, SparseCore 0:
  107.5 199.1 all-gather.2
where the time goes:
time: 338 us
  waiting for transfers between devices  216 us (64%)
  starting transfers between devices  36.3 us (11%)
  local copies, waits for them, and re-layouts  35.2 us (10%)
  matrix products  23.9 us (7%)
  between operations  14.5 us (4%)
  other arithmetic  11.6 us (3%)
    all_gather x1, waiting for transfers between devices, shards(): ctx_all = lax.all_gather(context[None], COL + (DEP,), axis=0, tiled=True)  112 us
    ppermute x14, waiting for transfers between devices, shift(): return lax.ppermute(x, axis, [(i, (i + s) % n) for i in range(n)])  66.8 us
    ppermute x6, waiting for transfers between devices, shift_open(): lax.ppermute(x, axis, [(i, i + s) for i in range(n) if 0 <= i + s < n])  36.9 us
    ppermute x14, starting transfers between devices, shift(): return lax.ppermute(x, axis, [(i, (i + s) % n) for i in range(n)])  21.9 us
    ppermute x6, starting transfers between devices, shift_open(): lax.ppermute(x, axis, [(i, i + s) for i in range(n) if 0 <= i + s < n])  14.4 us
    unnamed x45, local copies, waits for them, and re-layouts  13 us
    reshape x1, local copies, waits for them, and re-layouts, shards(): ctx_all = ctx_all.reshape(n_zh * n_x * n_core, n_dep * tok_depth, head_dim)  12.4 us
    dot_general x1, matrix products, shards(): jnp.einsum('ntk,tf->nkf', ctx_all, rows_all, preferred_element_type=jnp.f...  11.8 us
  transfers between devices with their start and end apart: 21, of which 17 were waited for; matrix products, arithmetic and copies ran while one was open for 5% of the time, Pallas kernels for 0%

commit v1 on v0

--- a/solution.py
+++ b/solution.py
@@ -9,6 +9,13 @@
 FAR = 1 << 30
 COL = ("zh", "x", "core")
 DEP = "zl"
+
+
+def exchange_gather(block, name, dim):
+    size = lax.axis_size(name)
+    parts = jnp.stack([block for _ in range(size)])
+    parts = lax.all_to_all(parts, name, split_axis=0, concat_axis=0)
+    return jnp.concatenate(parts, axis=dim)
 
 
 def segment_count(positions, seg_ends):
@@ -93,7 +100,7 @@
             jnp.bfloat16
         )
         context = roll_rows(context, -me_r * n_tok, 0)
-        ctx_all = lax.all_gather(context[None], COL + (DEP,), axis=0, tiled=True)
+        ctx_all = exchange_gather(context[None], COL + (DEP,), 0)
         ctx_all = ctx_all.reshape(n_zh * n_x * n_core, n_dep * tok_depth, head_dim)
         grad_prob = jnp.dot(context_grad, values_all.T, preferred_element_type=jnp.float32)
         delta_row = jnp.sum(prob_full * grad_prob, axis=1, keepdims=True)

time: 338 us -> 412 us (1.22)
  the two profiles are of different devices: /device:TPU:96 before, /device:TPU:1 now
where the time goes in v1:
time: 412 us; the launch traced here: 411 us
  waiting for transfers between devices  278 us (67%)
  starting transfers between devices  56.8 us (14%)
  local copies, waits for them, and re-layouts  40.3 us (10%)
  matrix products  23.9 us (6%)
  other arithmetic  11 us (3%)
    ppermute x14, waiting for transfers between devices, shift(): return lax.ppermute(x, axis, [(i, (i + s) % n) for i in range(n)])  250 us
    ppermute x6, waiting for transfers between devices, shift_open(): lax.ppermute(x, axis, [(i, i + s) for i in range(n) if 0 <= i + s < n])  27.5 us
    ppermute x14, starting transfers between devices, shift(): return lax.ppermute(x, axis, [(i, (i + s) % n) for i in range(n)])  23.8 us
    all_to_all x1, starting transfers between devices, exchange_gather(): parts = lax.all_to_all(parts, name, split_axis=0, concat_axis=0)  17.9 us
    ppermute x6, starting transfers between devices, shift_open(): lax.ppermute(x, axis, [(i, i + s) for i in range(n) if 0 <= i + s < n])  15 us
    unnamed x45, local copies, waits for them, and re-layouts  12.9 us
    dot_general x1, local copies, waits for them, and re-layouts, shards(): jnp.einsum('ntk,tf->nkf', ctx_all, rows_all, preferred_element_type=jnp.f...  12.3 us
    dot_general x1, matrix products, shards(): jnp.einsum('ntk,tf->nkf', ctx_all, rows_all, preferred_element_type=jnp.f...  11.8 us
  transfers between devices with their start and end apart: 21, of which 14 were waited for; matrix products, arithmetic and copies ran while one was open for 4% of the time, Pallas kernels for 0%

profile of v1, /device:TPU:1, one launch (start us, length us, event | category | flops | bytes accessed | tf_op | source)
XLA Modules:
  0.0 411.0 jit_solution(14538623817890356671)
XLA Ops:
  2.9 2.6 collective-permute-start.10
  7.6 6.6 %collective-permute-done.10 = bf16[128,768]{1,0:T(8,128)(2,1)S(1)} collective-permute-done((bf16[128,768]{1,0:T(8,128)(2,1)}, bf16[128,768]{1,0:T(8,128)(2,1)S(1)}, u32[]{:S(2)}, u32[]{:S(2)}) %collective-permute-start.10) | collective-permute-done | bytes 196640 | tf_op jit(solution)/shard_map/ppermute | solution.py:26
  15.3 3.1 fusion.1
  18.5 3.2 reshape.111
  21.7 6.3 %constant_dynamic-slice_fusion.1 = (bf16[2,4,1,128,512]{3,2,1,0,4:T(2,128)(2,1)}, bf16[2,4,1,128,512]{3,2,1,0,4:T(2,128)(2,1)}) fusion(bf16[2,4,2,128,512]{3,2,1,0,4:T(2,128)(2,1)S(1)} %reshape.111, s32[]{:T(128)S(6)} %select_n.93, s32[]{:T(128)S(6)} %select_n.95), kind=kLoop, calls=%fused_computation.71 | loop fusion | bytes 4194312 | tf_op jit(solution)/shard_map/jit(dynamic_index_in_dim)/dynamic_slice | solution.py:46
  28.1 6.0 %copy.51 = bf16[2,4,1,128,512]{4,3,1,0,2:T(8,128)(2,1)} copy(bf16[2,4,1,128,512]{3,2,1,0,4:T(2,128)(2,1)} %get-tuple-element.27) | data formatting | bytes 2097152
  35.7 7.0 %collective-permute-start.2 = (bf16[512,256]{1,0:T(8,128)(2,1)S(1)}, bf16[512,256]{1,0:T(8,128)(2,1)}, u32[]{:S(2)}, u32[]{:S(2)}) collective-permute-start(bf16[512,256]{1,0:T(8,128)(2,1)S(1)} %constant_dynamic-update-slice_fusion), channel_id=1, source_target_pairs={{0,3},{4,7},{8,11},{12,15},{16,19},{20,23},{24,27},{28,31},{32,35}... | collective-permute-start | bytes 786440 | tf_op jit(solution)/shard_map/ppermute | solution.py:30
  50.6 2.8 collective-permute-done.1
  53.4 5.6 %collective-permute-done = bf16[512,256]{1,0:T(8,128)(2,1)} collective-permute-done((bf16[512,256]{1,0:T(8,128)(2,1)S(1)}, bf16[512,256]{1,0:T(8,128)(2,1)}, u32[]{:S(2)}, u32[]{:S(2)}) %collective-permute-start) | collective-permute-done | bytes 262176 | tf_op jit(solution)/shard_map/ppermute | solution.py:30
  67.6 3.0 collective-permute-done.13
  70.6 6.6 %collective-permute-done.14 = bf16[2,128,512]{2,1,0:T(8,128)(2,1)S(1)} collective-permute-done((bf16[2,128,512]{2,1,0:T(8,128)(2,1)S(1)}, bf16[2,128,512]{2,1,0:T(8,128)(2,1)S(1)}, u32[]{:S(2)}, u32[]{:S(2)}) %collective-permute-start.14) | collective-permute-done | bytes 262176 | tf_op jit(solution)/shard_map/ppermute | solution.py:26
  77.4 4.3 %collective-permute-start.16 = (bf16[128,512]{1,0:T(8,128)(2,1)S(1)}, bf16[128,512]{1,0:T(8,128)(2,1)S(1)}, u32[]{:S(2)}, u32[]{:S(2)}) collective-permute-start(bf16[128,512]{1,0:T(8,128)(2,1)S(1)} %dynamic-slice_bitcast_fusion.3), channel_id=1, source_target_pairs={{0,32},{32,0},{1,33},{33,1},{2,34},{34,2},{3,35},{35,3},{4,36},{36... | collective-permute-start | bytes 393224 | tf_op jit(solution)/shard_map/ppermute | solution.py:26
  85.2 4.0 multiply_reduce_fusion
  91.7 5.2 %stack.60 = bf16[64,1,512,128]{3,2,1,0:T(8,128)(2,1)} broadcast(bf16[512,128]{1,0:T(8,128)(2,1)S(1)} %fusion.24), dimensions={2,3} | broadcast | bytes 8519680 | tf_op jit(solution)/shard_map/stack | solution.py:16
  96.9 17.9 %all-to-all-start = ((bf16[64,1,512,128]{3,2,1,0:T(8,128)(2,1)}), bf16[64,1,512,128]{3,2,1,0:T(8,128)(2,1)}, u32[]{:S(2)}, u32[]{:S(2)}) async-start(bf16[64,1,512,128]{3,2,1,0:T(8,128)(2,1)} %stack.60), calls=%async_computation | async-start | bytes 16777216 | tf_op jit(solution)/shard_map/all_to_all | solution.py:17
  114.9 3.3 collective-permute-start.3
  118.7 182.6 %collective-permute-done.3 = bf16[128,768]{1,0:T(8,128)(2,1)S(1)} collective-permute-done((bf16[128,768]{1,0:T(8,128)(2,1)S(1)}, bf16[128,768]{1,0:T(8,128)(2,1)S(1)}, u32[]{:S(2)}, u32[]{:S(2)}) %collective-permute-start.3) | collective-permute-done | bytes 196640 | tf_op jit(solution)/shard_map/ppermute | solution.py:26
  301.3 15.0 %collective-permute-done.4 = bf16[128,768]{1,0:T(8,128)(2,1)S(1)} collective-permute-done((bf16[128,768]{1,0:T(8,128)(2,1)S(1)}, bf16[128,768]{1,0:T(8,128)(2,1)S(1)}, u32[]{:S(2)}, u32[]{:S(2)}) %collective-permute-start.4) | collective-permute-done | bytes 196640 | tf_op jit(solution)/shard_map/ppermute | solution.py:26
  320.6 15.8 %collective-permute-done.7 = bf16[4,128,768]{2,1,0:T(8,128)(2,1)S(1)} collective-permute-done((bf16[4,128,768]{2,1,0:T(8,128)(2,1)S(1)}, bf16[4,128,768]{2,1,0:T(8,128)(2,1)S(1)}, u32[]{:S(2)}, u32[]{:S(2)}) %collective-permute-start.7) | collective-permute-done | bytes 786464 | tf_op jit(solution)/shard_map/ppermute | solution.py:26
  336.4 16.7 %collective-permute-done.6 = bf16[4,128,768]{2,1,0:T(8,128)(2,1)S(1)} collective-permute-done((bf16[4,128,768]{2,1,0:T(8,128)(2,1)S(1)}, bf16[4,128,768]{2,1,0:T(8,128)(2,1)S(1)}, u32[]{:S(2)}, u32[]{:S(2)}) %collective-permute-start.6) | collective-permute-done | bytes 786464 | tf_op jit(solution)/shard_map/ppermute | solution.py:26
  366.1 10.6 %collective-permute-done.17 = bf16[512,256]{0,1:T(8,128)(2,1)S(1)} collective-permute-done((bf16[512,256]{0,1:T(8,128)(2,1)S(1)}, bf16[512,256]{0,1:T(8,128)(2,1)S(1)}, u32[]{:S(2)}, u32[]{:S(2)}) %collective-permute-start.17) | collective-permute-done | bytes 262176 | tf_op jit(solution)/shard_map/ppermute | solution.py:30
  376.7 8.5 %collective-permute-done.18 = bf16[512,256]{0,1:T(8,128)(2,1)S(1)} collective-permute-done((bf16[512,256]{0,1:T(8,128)(2,1)S(1)}, bf16[512,256]{0,1:T(8,128)(2,1)S(1)}, u32[]{:S(2)}, u32[]{:S(2)}) %collective-permute-start.18) | collective-permute-done | bytes 262176 | tf_op jit(solution)/shard_map/ppermute | solution.py:30
  386.9 12.3 %copy.40 = bf16[16,128,2048]{2,1,0:T(8,128)(2,1)} copy(bf16[16,128,2048]{1,2,0:T(8,128)(2,1)} %bitcast.9) | data formatting | bytes 16777216 | tf_op jit(solution)/shard_map/ntk,tf->nkf/dot_general | solution.py:129
  399.2 11.8 %fusion.29 = f32[2048,768]{1,0:T(8,128)} fusion(bf16[2048,2048]{1,0:T(8,128)(2,1)} %bitcast.81, bf16[2048,768]{1,0:T(8,128)(2,1)} %bitcast.82), kind=kOutput, calls=%fused_computation.76 | convolution fusion | flops 6442450944 | bytes 17825792 | tf_op jit(solution)/shard_map/ntk,tf->nkf/dot_general | solution.py:129
  (99 shorter events, 49.1 us)
Async XLA Ops:
  0.6 6.9 %collective-permute-start.11 = (bf16[128,768]{1,0:T(8,128)(2,1)}, bf16[128,768]{1,0:T(8,128)(2,1)S(1)}, u32[]{:S(2)}, u32[]{:S(2)}) collective-permute-start(bf16[128,768]{1,0:T(8,128)(2,1)} %bitcast.87), channel_id=1, source_target_pairs={{0,64},{64,128},{128,192},{192,0},{1,65},{65,129},{129,193},{193,1... | collective-permute-start | bytes 589832 | tf_op jit(solution)/shard_map/ppermute | solution.py:26
  2.9 11.3 %collective-permute-start.10 = (bf16[128,768]{1,0:T(8,128)(2,1)}, bf16[128,768]{1,0:T(8,128)(2,1)S(1)}, u32[]{:S(2)}, u32[]{:S(2)}) collective-permute-start(bf16[128,768]{1,0:T(8,128)(2,1)} %bitcast.88), channel_id=1, source_target_pairs={{0,128},{64,192},{128,0},{192,64},{1,129},{65,193},{129,1},{193,65... | collective-permute-start | bytes 589832 | tf_op jit(solution)/shard_map/ppermute | solution.py:26
  5.5 8.7 %collective-permute-start.9 = (bf16[128,768]{1,0:T(8,128)(2,1)}, bf16[128,768]{1,0:T(8,128)(2,1)}, u32[]{:S(2)}, u32[]{:S(2)}) collective-permute-start(bf16[128,768]{1,0:T(8,128)(2,1)} %bitcast.89), channel_id=1, source_target_pairs={{0,192},{64,0},{128,64},{192,128},{1,193},{65,1},{129,65},{193,129... | collective-permute-start | bytes 589832 | tf_op jit(solution)/shard_map/ppermute | solution.py:26
  28.1 19.9 %copy-start.4 = (bf16[2,4,1,128,512]{3,2,1,0,4:T(2,128)(2,1)S(1)}, bf16[2,4,1,128,512]{3,2,1,0,4:T(2,128)(2,1)}, u32[]{:S(2)}) copy-start(bf16[2,4,1,128,512]{3,2,1,0,4:T(2,128)(2,1)} %get-tuple-element.26) | copy-start | bytes 3145732
  34.1 26.2 %collective-permute-start.12 = (bf16[2,4,128,512]{3,2,1,0:T(8,128)(2,1)}, bf16[2,4,128,512]{3,2,1,0:T(8,128)(2,1)}, u32[]{:S(2)}, u32[]{:S(2)}) collective-permute-start(bf16[2,4,128,512]{3,2,1,0:T(8,128)(2,1)} %bitcast.28), channel_id=1, source_target_pairs={{0,4},{4,0},{1,5},{5,1},{2,6},{6,2},{3,7},{7,3},{8,12},{12,8},{9,1... | collective-permute-start | bytes 3145736 | tf_op jit(solution)/shard_map/ppermute | solution.py:26
  35.7 14.9 %collective-permute-start.2 = (bf16[512,256]{1,0:T(8,128)(2,1)S(1)}, bf16[512,256]{1,0:T(8,128)(2,1)}, u32[]{:S(2)}, u32[]{:S(2)}) collective-permute-start(bf16[512,256]{1,0:T(8,128)(2,1)S(1)} %constant_dynamic-update-slice_fusion), channel_id=1, source_target_pairs={{0,3},{4,7},{8,11},{12,15},{16,19},{20,23},{24,27},{28,31},{32,35}... | collective-permute-start | bytes 786440 | tf_op jit(solution)/shard_map/ppermute | solution.py:30
  42.7 10.7 %collective-permute-start.1 = (bf16[512,256]{1,0:T(8,128)(2,1)S(1)}, bf16[512,256]{1,0:T(8,128)(2,1)}, u32[]{:S(2)}, u32[]{:S(2)}) collective-permute-start(bf16[512,256]{1,0:T(8,128)(2,1)S(1)} %constant_dynamic-update-slice_fusion), channel_id=1, source_target_pairs={{0,2},{1,3},{4,6},{5,7},{8,10},{9,11},{12,14},{13,15},{16,18},{17,... | collective-permute-start | bytes 786440 | tf_op jit(solution)/shard_map/ppermute | solution.py:30
  44.6 14.3 %collective-permute-start = (bf16[512,256]{1,0:T(8,128)(2,1)S(1)}, bf16[512,256]{1,0:T(8,128)(2,1)}, u32[]{:S(2)}, u32[]{:S(2)}) collective-permute-start(bf16[512,256]{1,0:T(8,128)(2,1)S(1)} %constant_dynamic-update-slice_fusion), channel_id=1, source_target_pairs={{0,1},{1,2},{2,3},{4,5},{5,6},{6,7},{8,9},{9,10},{10,11},{12,13},{... | collective-permute-start | bytes 786440 | tf_op jit(solution)/shard_map/ppermute | solution.py:30
  60.3 29.0 %copy-start.6 = (bf16[4,512,256]{2,1,0:T(8,128)(2,1)}, bf16[4,512,256]{2,1,0:T(8,128)(2,1)S(1)}, u32[]{:S(2)}) copy-start(bf16[4,512,256]{2,1,0:T(8,128)(2,1)S(1)} %pad_maximum_fusion.1) | copy-start | bytes 3145732
  62.3 8.3 %collective-permute-start.13 = (bf16[2,128,512]{2,1,0:T(8,128)(2,1)S(1)}, bf16[2,128,512]{2,1,0:T(8,128)(2,1)S(1)}, u32[]{:S(2)}, u32[]{:S(2)}) collective-permute-start(bf16[2,128,512]{2,1,0:T(8,128)(2,1)S(1)} %get-tuple-element.31), channel_id=1, source_target_pairs={{0,8},{8,16},{16,24},{24,0},{1,9},{9,17},{17,25},{25,1},{2,10},{10... | collective-permute-start | bytes 786440 | tf_op jit(solution)/shard_map/ppermute | solution.py:26
  63.6 7.1 %collective-permute-start.15 = (bf16[2,128,512]{2,1,0:T(8,128)(2,1)S(1)}, bf16[2,128,512]{2,1,0:T(8,128)(2,1)S(1)}, u32[]{:S(2)}, u32[]{:S(2)}) collective-permute-start(bf16[2,128,512]{2,1,0:T(8,128)(2,1)S(1)} %get-tuple-element.32), channel_id=1, source_target_pairs={{0,24},{8,0},{16,8},{24,16},{1,25},{9,1},{17,9},{25,17},{2,26},{10... | collective-permute-start | bytes 786440 | tf_op jit(solution)/shard_map/ppermute | solution.py:26
  65.0 12.2 %collective-permute-start.14 = (bf16[2,128,512]{2,1,0:T(8,128)(2,1)S(1)}, bf16[2,128,512]{2,1,0:T(8,128)(2,1)S(1)}, u32[]{:S(2)}, u32[]{:S(2)}) collective-permute-start(bf16[2,128,512]{2,1,0:T(8,128)(2,1)S(1)} %get-tuple-element.33), channel_id=1, source_target_pairs={{0,16},{8,24},{16,0},{24,8},{1,17},{9,25},{17,1},{25,9},{2,18},{10... | collective-permute-start | bytes 786440 | tf_op jit(solution)/shard_map/ppermute | solution.py:26
  77.4 7.8 %collective-permute-start.16 = (bf16[128,512]{1,0:T(8,128)(2,1)S(1)}, bf16[128,512]{1,0:T(8,128)(2,1)S(1)}, u32[]{:S(2)}, u32[]{:S(2)}) collective-permute-start(bf16[128,512]{1,0:T(8,128)(2,1)S(1)} %dynamic-slice_bitcast_fusion.3), channel_id=1, source_target_pairs={{0,32},{32,0},{1,33},{33,1},{2,34},{34,2},{3,35},{35,3},{4,36},{36... | collective-permute-start | bytes 393224 | tf_op jit(solution)/shard_map/ppermute | solution.py:26
  96.9 290.0 %all-to-all-start = ((bf16[64,1,512,128]{3,2,1,0:T(8,128)(2,1)}), bf16[64,1,512,128]{3,2,1,0:T(8,128)(2,1)}, u32[]{:S(2)}, u32[]{:S(2)}) async-start(bf16[64,1,512,128]{3,2,1,0:T(8,128)(2,1)} %stack.60), calls=%async_computation | async-start | bytes 16777216 | tf_op jit(solution)/shard_map/all_to_all | solution.py:17
  114.9 186.4 %collective-permute-start.3 = (bf16[128,768]{1,0:T(8,128)(2,1)S(1)}, bf16[128,768]{1,0:T(8,128)(2,1)S(1)}, u32[]{:S(2)}, u32[]{:S(2)}) collective-permute-start(bf16[128,768]{1,0:T(8,128)(2,1)S(1)} %bitcast.90), channel_id=1, source_target_pairs={{0,3},{1,0},{2,1},{3,2},{4,7},{5,4},{6,5},{7,6},{8,11},{9,8},{10,9... | collective-permute-start | bytes 589832 | tf_op jit(solution)/shard_map/ppermute | solution.py:26
  118.1 198.2 %collective-permute-start.5 = (bf16[128,768]{1,0:T(8,128)(2,1)S(1)}, bf16[128,768]{1,0:T(8,128)(2,1)S(1)}, u32[]{:S(2)}, u32[]{:S(2)}) collective-permute-start(bf16[128,768]{1,0:T(8,128)(2,1)S(1)} %bitcast.91), channel_id=1, source_target_pairs={{0,1},{1,2},{2,3},{3,0},{4,5},{5,6},{6,7},{7,4},{8,9},{9,10},{10,1... | collective-permute-start | bytes 589832 | tf_op jit(solution)/shard_map/ppermute | solution.py:26
  118.1 198.2 %collective-permute-start.4 = (bf16[128,768]{1,0:T(8,128)(2,1)S(1)}, bf16[128,768]{1,0:T(8,128)(2,1)S(1)}, u32[]{:S(2)}, u32[]{:S(2)}) collective-permute-start(bf16[128,768]{1,0:T(8,128)(2,1)S(1)} %bitcast.92), channel_id=1, source_target_pairs={{0,2},{1,3},{2,0},{3,1},{4,6},{5,7},{6,4},{7,5},{8,10},{9,11},{10,... | collective-permute-start | bytes 589832 | tf_op jit(solution)/shard_map/ppermute | solution.py:26
  316.5 39.9 %copy-start.5 = (f32[512,2048]{0,1:T(8,128)S(1)}, f32[512,2048]{0,1:T(8,128)}, u32[]{:S(2)}) copy-start(f32[512,2048]{0,1:T(8,128)} %get-tuple-element.38) | copy-start | bytes 12582916
  316.6 19.8 %collective-permute-start.7 = (bf16[4,128,768]{2,1,0:T(8,128)(2,1)S(1)}, bf16[4,128,768]{2,1,0:T(8,128)(2,1)S(1)}, u32[]{:S(2)}, u32[]{:S(2)}) collective-permute-start(bf16[4,128,768]{2,1,0:T(8,128)(2,1)S(1)} %constant_dynamic-slice_fusion.2), channel_id=1, source_target_pairs={{0,128},{64,192},{128,0},{192,64},{1,129},{65,193},{129,1},{193,65... | collective-permute-start | bytes 2359304 | tf_op jit(solution)/shard_map/ppermute | solution.py:26
  319.1 34.0 %collective-permute-start.6 = (bf16[4,128,768]{2,1,0:T(8,128)(2,1)S(1)}, bf16[4,128,768]{2,1,0:T(8,128)(2,1)S(1)}, u32[]{:S(2)}, u32[]{:S(2)}) collective-permute-start(bf16[4,128,768]{2,1,0:T(8,128)(2,1)S(1)} %constant_dynamic-slice_fusion.2), channel_id=1, source_target_pairs={{0,192},{64,0},{128,64},{192,128},{1,193},{65,1},{129,65},{193,129... | collective-permute-start | bytes 2359304 | tf_op jit(solution)/shard_map/ppermute | solution.py:26
  320.1 34.4 %collective-permute-start.8 = (bf16[4,128,768]{2,1,0:T(8,128)(2,1)S(1)}, bf16[4,128,768]{2,1,0:T(8,128)(2,1)S(1)}, u32[]{:S(2)}, u32[]{:S(2)}) collective-permute-start(bf16[4,128,768]{2,1,0:T(8,128)(2,1)S(1)} %constant_dynamic-slice_fusion.2), channel_id=1, source_target_pairs={{0,64},{64,128},{128,192},{192,0},{1,65},{65,129},{129,193},{193,1... | collective-permute-start | bytes 2359304 | tf_op jit(solution)/shard_map/ppermute | solution.py:26
  360.8 15.9 %collective-permute-start.17 = (bf16[512,256]{0,1:T(8,128)(2,1)S(1)}, bf16[512,256]{0,1:T(8,128)(2,1)S(1)}, u32[]{:S(2)}, u32[]{:S(2)}) collective-permute-start(bf16[512,256]{0,1:T(8,128)(2,1)S(1)} %get-tuple-element.28), channel_id=1, source_target_pairs={{1,0},{2,1},{3,2},{5,4},{6,5},{7,6},{9,8},{10,9},{11,10},{13,12},{... | collective-permute-start | bytes 786440 | tf_op jit(solution)/shard_map/ppermute | solution.py:30
  362.1 14.7 %collective-permute-start.19 = (bf16[512,256]{0,1:T(8,128)(2,1)S(1)}, bf16[512,256]{0,1:T(8,128)(2,1)S(1)}, u32[]{:S(2)}, u32[]{:S(2)}) collective-permute-start(bf16[512,256]{0,1:T(8,128)(2,1)S(1)} %get-tuple-element.29), channel_id=1, source_target_pairs={{3,0},{7,4},{11,8},{15,12},{19,16},{23,20},{27,24},{31,28},{35,32}... | collective-permute-start | bytes 786440 | tf_op jit(solution)/shard_map/ppermute | solution.py:30
  363.4 21.9 %collective-permute-start.18 = (bf16[512,256]{0,1:T(8,128)(2,1)S(1)}, bf16[512,256]{0,1:T(8,128)(2,1)S(1)}, u32[]{:S(2)}, u32[]{:S(2)}) collective-permute-start(bf16[512,256]{0,1:T(8,128)(2,1)S(1)} %get-tuple-element.30), channel_id=1, source_target_pairs={{2,0},{3,1},{6,4},{7,5},{10,8},{11,9},{14,12},{15,13},{18,16},{19,... | collective-permute-start | bytes 786440 | tf_op jit(solution)/shard_map/ppermute | solution.py:30
  (13 other events, 123.4 us)
